TPU v7x, 256 devices: a whole 4x4x8 slice. The times are simulated.
256 devices in a mesh: row: 16 (over z, y_hi), col: 16 (over x, y_lo, core).
Axes of the slice: x: 4, y: 4 (y_hi: 2, y_lo: 2; y = y_hi * 2 + y_lo), z: 8, core: 2. Of those that a mesh axis runs over, the one named last changes fastest.
Arguments:
- features: bfloat16 [512, 512, 256], P('row', 'col'), may hold values from -6 to 6
- dw_kernel: bfloat16 [7, 7, 256], replicated, may hold values from -0.875 to 0.875
- dw_bias: float32 [256], replicated, may hold values from -4 to 4
- norm_gain: float32 [256], replicated, may hold values from 0.5 to 2
- norm_bias: float32 [256], replicated, may hold values from -3 to 3
- w_expand: bfloat16 [256, 1024], replicated, may hold values from -0.375 to 0.375
- b_expand: float32 [1024], replicated, may hold values from -3 to 3
- w_reduce: bfloat16 [1024, 256], replicated, may hold values from -0.1875 to 0.1875
- b_reduce: float32 [256], replicated, may hold values from -3 to 3
- layer_scale: float32 [256], replicated, may hold values from 0.5 to 2
- w_query: bfloat16 [256, 256], replicated, may hold values from -2 to 2
- w_keyval: bfloat16 [256, 512], replicated, may hold values from -0.375 to 0.375
- rel_bias: float32 [8, 7, 127], replicated, may hold values from -8 to 250, as said below
- w_out: bfloat16 [256, 256], replicated, may hold values from -0.75 to 0.75
Outputs:
- result: bfloat16 [512, 512, 256], P('row', 'col')
Inputs may be any that keep to these rules, and one draw needn't show every extreme that they name: `rel_bias`: relative position bias of moderate size, with possibly a few much larger entries.
All inputs are finite; a program needn't handle non-finite values.
Results may differ from a plain program's by a relative error of at most 0.014.
Values may be sent and summed in bfloat16 or wider, within the bound.
No kernel may reach another device: no remote copies, remote signals or barrier semaphores. Data moves between devices by JAX's collectives and lax.ppermute only.
A program may use at most 64 MiB of HBM per device.

v0:
```python
import jax
import jax.numpy as jnp
from jax import lax
from jax.sharding import PartitionSpec as P

HEADS = 8


def padded_2(array, sides, width):
    for axis, dim in sides:
        devices, length = (lax.axis_size(axis), array.shape[dim])
        up = [(i, (i + 1) % devices) for i in range(devices - 1)]
        down = [(j, i) for i, j in up]
        last = lax.slice_in_dim(array, length - width, length, axis=dim)
        leading = lax.slice_in_dim(array, 0, width, axis=dim)
        before = lax.ppermute(last, axis, up)
        after = lax.ppermute(leading, axis, down)
        array = jnp.concatenate([before, array, after], axis=dim)
    return array


def block_pass(
    padded,
    features,
    dw_kernel,
    dw_bias,
    norm_gain,
    norm_bias,
    w_expand,
    b_expand,
    w_reduce,
    b_reduce,
    layer_scale,
):
    tile_rows, tile_cols, channels = features.shape
    convolved = jnp.zeros((tile_rows, tile_cols, channels), jnp.float32)
    for tap_row in range(7):
        for tap_col in range(7):
            convolved = convolved + padded[
                tap_row : tap_row + tile_rows, tap_col : tap_col + tile_cols
            ].astype(jnp.float32) * dw_kernel[tap_row, tap_col].astype(jnp.float32)
    convolved = convolved + dw_bias
    average = jnp.mean(convolved, axis=-1, keepdims=True)
    centred = convolved - average
    variance = jnp.mean(centred * centred, axis=-1, keepdims=True)
    normed = (
        (centred * lax.rsqrt(variance + 1e-06) * norm_gain + norm_bias)
        .astype(jnp.bfloat16)
        .reshape(-1, channels)
    )
    hidden = jax.nn.gelu(
        jnp.dot(normed, w_expand, preferred_element_type=jnp.float32) + b_expand, approximate=False
    ).astype(jnp.bfloat16)
    reduced = jnp.dot(hidden, w_reduce, preferred_element_type=jnp.float32) + b_reduce
    summed = features.astype(jnp.float32).reshape(-1, channels) + layer_scale * reduced
    return summed.astype(jnp.bfloat16).reshape(tile_rows, tile_cols, channels)


def shards(
    features,
    dw_kernel,
    dw_bias,
    norm_gain,
    norm_bias,
    w_expand,
    b_expand,
    w_reduce,
    b_reduce,
    layer_scale,
    w_query,
    w_keyval,
    rel_bias,
    w_out,
):
    tile_rows, tile_cols, channels = features.shape
    head_dim = channels // HEADS
    extended = padded_2(features, (("row", 0),), 3)
    padded = padded_2(extended, (("col", 1),), 3)
    block_out = block_pass(
        padded,
        features,
        dw_kernel,
        dw_bias,
        norm_gain,
        norm_bias,
        w_expand,
        b_expand,
        w_reduce,
        b_reduce,
        layer_scale,
    )
    region_side = tile_rows // 8
    local_count = region_side * region_side
    pooled = (
        block_out.astype(jnp.float32)
        .reshape(region_side, 8, region_side, 8, channels)
        .mean(axis=(1, 3))
    )
    pooled = pooled.astype(jnp.bfloat16).reshape(local_count, channels)
    queries = jnp.dot(pooled, w_query, preferred_element_type=jnp.float32).astype(jnp.bfloat16)
    keyval = jnp.dot(pooled, w_keyval, preferred_element_type=jnp.float32).astype(jnp.bfloat16)
    band_keyval = lax.all_gather(keyval, "col", axis=0, tiled=True)
    columns = lax.axis_size("col")
    position = lax.axis_index("col")
    span_cols = region_side * columns
    key_count = local_count * columns
    side_index = jnp.arange(region_side, dtype=jnp.int32)
    row_offsets = side_index[None, :] - side_index[:, None] + region_side - 1
    row_onehot = (
        row_offsets[:, :, None] == jnp.arange(2 * region_side - 1, dtype=jnp.int32)[None, None, :]
    ).astype(jnp.float32)
    row_picked = jnp.einsum("rso,hoc->hrsc", row_onehot, rel_bias, precision=lax.Precision.HIGHEST)
    query_cols = position * region_side + side_index
    span_index = jnp.arange(span_cols, dtype=jnp.int32)
    col_offsets = span_index[None, :] - query_cols[:, None] + span_cols - 1
    col_onehot = (
        col_offsets[:, :, None] == jnp.arange(2 * span_cols - 1, dtype=jnp.int32)[None, None, :]
    ).astype(jnp.float32)
    both_picked = jnp.einsum(
        "hrsc,qkc->hrqsk", row_picked, col_onehot, precision=lax.Precision.HIGHEST
    )
    both_picked = both_picked.reshape(
        HEADS, region_side, region_side, region_side, columns, region_side
    )
    bias_block = jnp.transpose(both_picked, (0, 1, 2, 4, 3, 5)).reshape(
        HEADS, local_count, key_count
    )
    query_heads = queries.reshape(local_count, HEADS, head_dim)
    key_heads = band_keyval[:, :channels].reshape(key_count, HEADS, head_dim)
    value_heads = band_keyval[:, channels:].reshape(key_count, HEADS, head_dim)
    scores = (
        jnp.einsum("qhd,khd->hqk", query_heads, key_heads, preferred_element_type=jnp.float32)
        / jnp.sqrt(jnp.float32(head_dim))
        + bias_block
    )
    attn = jax.nn.softmax(scores, axis=-1).astype(jnp.bfloat16)
    context = (
        jnp.einsum("hqk,khd->qhd", attn, value_heads, preferred_element_type=jnp.float32)
        .reshape(local_count, channels)
        .astype(jnp.bfloat16)
    )
    lifted = jnp.dot(context, w_out, preferred_element_type=jnp.float32).reshape(
        region_side, 1, region_side, 1, channels
    )
    spread = jnp.broadcast_to(lifted, (region_side, 8, region_side, 8, channels)).reshape(
        tile_rows, tile_cols, channels
    )
    return (block_out.astype(jnp.float32) + spread).astype(jnp.bfloat16)


def solution(mesh):
    return jax.shard_map(
        shards,
        mesh=mesh,
        in_specs=(
            P("row", "col", None),
            P(),
            P(),
            P(),
            P(),
            P(),
            P(),
            P(),
            P(),
            P(),
            P(),
            P(),
            P(),
            P(),
        ),
        out_specs=P("row", "col", None),
        check_vma=False,
    )
```

profile of v0, /device:TPU:129, one launch (start us, length us, event | category | flops | bytes accessed | tf_op | source)
XLA Modules:
  0.0 78.3 jit_solution(13312583361902755873)
XLA Ops:
  0.0 0.9 %fusion.106 = (bf16[3,32,256]{2,1,0:T(8,128)(2,1)S(1)}, bf16[3,32,256]{2,1,0:T(8,128)(2,1)S(1)}) fusion(bf16[32,32,256]{2,1,0:T(8,128)(2,1)} %param.14), kind=kLoop, calls=%fused_computation.266 | loop fusion | bytes 196608 | tf_op jit(solution)/shard_map/slice | solution.py:15
  0.9 4.8 %collective-permute-start = (bf16[3,32,256]{2,1,0:T(8,128)(2,1)S(1)}, bf16[3,32,256]{2,1,0:T(8,128)(2,1)S(1)}, u32[]{:S(2)}, u32[]{:S(2)}) collective-permute-start(bf16[3,32,256]{2,1,0:T(8,128)(2,1)S(1)} %get-tuple-element.13), channel_id=1, source_target_pairs={{0,16},{16,32},{32,48},{48,64},{64,80},{80,96},{96,112},{112,128},... | collective-permute-start | bytes 147464 | tf_op jit(solution)/shard_map/ppermute | solution.py:16
  5.7 4.1 %collective-permute-start.1 = (bf16[3,32,256]{2,1,0:T(8,128)(2,1)S(1)}, bf16[3,32,256]{2,1,0:T(8,128)(2,1)S(1)}, u32[]{:S(2)}, u32[]{:S(2)}) collective-permute-start(bf16[3,32,256]{2,1,0:T(8,128)(2,1)S(1)} %get-tuple-element.12), channel_id=1, source_target_pairs={{16,0},{32,16},{48,32},{64,48},{80,64},{96,80},{112,96},{128,112},... | collective-permute-start | bytes 147464 | tf_op jit(solution)/shard_map/ppermute | solution.py:17
  9.8 1.6 %slice_convert_fusion.48 = (f32[1,1,256]{2,1,0:T(1,128)S(1)}, f32[1,1,256]{2,1,0:T(1,128)S(1)}, f32[1,1,256]{2,1,0:T(1,128)S(1)}, f32[1,1,256]{2,1,0:T(1,128)S(1...) fusion(bf16[7,7,256]{2,1,0:T(8,128)(2,1)} %param.15), kind=kLoop, calls=%fused_computation.231 | loop fusion | flops 4864 | bytes 29184 | tf_op jit(solution)/shard_map/mul | solution.py:39
  11.5 1.0 %fusion.67 = f32[4,4,8,127]{3,1,2,0:T(4,128)S(1)} fusion(f32[8,7,127,1]{2,0,1,3:T(8,128)} %bitcast.105, s32[4,4]{1,0:T(4,128)S(1)} %subtract_add_fusion), kind=kOutput, calls=%fused_computation.165 | convolution fusion | flops 1365616 | bytes 93536 | tf_op jit(solution)/shard_map/rso,hoc->hrsc/dot_general | solution.py:112
  12.5 0.4 convolution_bitcast_fusion
  12.9 1.7 %slice_convert_fusion.47 = (f32[1,1,256]{2,1,0:T(1,128)}, f32[1,1,256]{2,1,0:T(1,128)}, f32[1,1,256]{2,1,0:T(1,128)}, f32[1,1,256]{2,1,0:T(1,128)}, f32[1,1,256]...) fusion(bf16[7,7,256]{2,1,0:T(8,128)(2,1)} %param.15), kind=kLoop, calls=%fused_computation.230 | loop fusion | flops 4864 | bytes 29184 | tf_op jit(solution)/shard_map/mul | solution.py:39
  14.6 1.2 %constant_dynamic-update-slice_fusion.3 = (bf16[35,32,256]{2,1,0:T(8,128)(2,1)S(1)}, bf16[38,32,256]{2,1,0:T(8,128)(2,1)S(1)}, bf16[35,32,256]{2,1,0:T(8,128)(2,1)S(1)}) fusion(bf16[35,32,256]{2,1,0:T(8,128)(2,1)S(1)} %get-tuple-element.16, bf16[32,32,256]{2,1,0:T(8,128)(2,1)} %param.14, bf16[38,32,256]{2,1,0:T(8,128)(2,1)S(1)} %get-tuple-element.17), kind=kLoop, calls=%fused_computation.171 | loop fusion | bytes 2097152 | tf_op jit(solution)/shard_map/concatenate | solution.py:18
  15.9 0.9 %fusion.105 = (bf16[38,3,256]{2,1,0:T(4,128)(2,1)}, bf16[38,3,256]{2,1,0:T(4,128)(2,1)}) fusion(bf16[38,32,256]{2,1,0:T(8,128)(2,1)S(1)} %get-tuple-element.19), kind=kLoop, calls=%fused_computation.265 | loop fusion | bytes 233472 | tf_op jit(solution)/shard_map/slice | solution.py:14
  16.8 3.1 %collective-permute-start.3 = (bf16[38,3,256]{2,1,0:T(4,128)(2,1)}, bf16[38,3,256]{2,1,0:T(4,128)(2,1)S(1)}, u32[]{:S(2)}, u32[]{:S(2)}) collective-permute-start(bf16[38,3,256]{2,1,0:T(4,128)(2,1)} %get-tuple-element.8), channel_id=1, source_target_pairs={{1,0},{2,1},{3,2},{4,3},{5,4},{6,5},{7,6},{8,7},{9,8},{10,9},{11,1... | collective-permute-start | bytes 175112 | tf_op jit(solution)/shard_map/ppermute | solution.py:17
  19.9 3.1 %collective-permute-start.2 = (bf16[38,3,256]{2,1,0:T(4,128)(2,1)}, bf16[38,3,256]{2,1,0:T(4,128)(2,1)}, u32[]{:S(2)}, u32[]{:S(2)}) collective-permute-start(bf16[38,3,256]{2,1,0:T(4,128)(2,1)} %get-tuple-element.7), channel_id=1, source_target_pairs={{0,1},{1,2},{2,3},{3,4},{4,5},{5,6},{6,7},{7,8},{8,9},{9,10},{10,1... | collective-permute-start | bytes 175112 | tf_op jit(solution)/shard_map/ppermute | solution.py:16
  23.0 1.5 %slice_convert_fusion.46 = (f32[1,1,256]{2,1,0:T(1,128)}, f32[1,1,256]{2,1,0:T(1,128)}, f32[1,1,256]{2,1,0:T(1,128)}, f32[1,1,256]{2,1,0:T(1,128)}, f32[1,1,256]...) fusion(bf16[7,7,256]{2,1,0:T(8,128)(2,1)} %param.15), kind=kLoop, calls=%fused_computation.229 | loop fusion | flops 2816 | bytes 16896 | tf_op jit(solution)/shard_map/mul | solution.py:39
  24.5 0.6 copy.22
  25.1 1.8 %copy.23 = f32[8,4,4,16,4,4]{0,5,4,3,2,1:T(4,128)} copy(f32[8,4,4,16,4,4]{0,5,3,4,2,1:T(4,128)S(1)} %bitcast.96) | data formatting | bytes 262144 | tf_op jit(solution)/shard_map/transpose | solution.py:125
  27.3 2.5 %copy.24 = f32[8,16,256]{2,1,0:T(8,128)S(1)} copy(f32[8,16,256]{0,2,1:T(8,128)} %bitcast.97) | data formatting | bytes 262144 | tf_op jit(solution)/shard_map/reshape | solution.py:125
  30.2 13.4 %fusion.104 = (f32[32,32]{1,0:T(8,128)S(1)}, f32[32,32,256]{2,1,0:T(8,128)S(1)}) fusion(f32[256]{0:T(256)} %param.16, f32[256]{0:T(256)} %bitcast.153, bf16[38,3,256]{2,1,0:T(4,128)(2,1)S(1)} %collective-permute-done.3, bf16[38,32,256]{2,1,0:T(8,128)(2,1)S(1)} %copy-done.5, f32[256]{0:T(256)} %bitcast.154, f32[256]{0:T(256)S(1)} %bitcast.107, ...), kind=kLoop, calls=%fused_computation.264 | loop fusion | flops 71826432 | bytes 5513216 | tf_op jit(solution)/shard_map/reduce_sum | solution.py:43
  43.6 0.4 multiply_reduce_fusion
  44.0 1.0 %add_convert_fusion.1 = bf16[32,32,256]{2,1,0:T(8,128)(2,1)S(1)} fusion(f32[32,32,256]{2,1,0:T(8,128)S(1)} %get-tuple-element.6, f32[256]{0:T(256)} %param.18, f32[256]{0:T(256)} %param.17, f32[32,32]{1,0:T(8,128)S(1)} %add_rsqrt_fusion, f32[32,32]{1,0:T(8,128)S(1)} %broadcast_multiply_fusion), kind=kLoop, calls=%fused_computation.75 | loop fusion | flops 1310720 | bytes 1583104 | tf_op jit(solution)/shard_map/convert_element_type | solution.py:48
  45.1 10.9 %fusion.14 = f32[1024,256]{1,0:T(8,128)S(1)} fusion(bf16[1024,256]{1,0:T(8,128)(2,1)S(1)} %copy-done, bf16[1024,256]{1,0:T(8,128)(2,1)S(1)} %bitcast.102, bf16[256,1024]{1,0:T(8,128)(2,1)} %param.19, f32[1024]{0:T(1024)S(1)} %copy-done.45, f32[256]{0:T(256)S(1)} %copy-done.46, f32[256]{0:T(256)S(1)} %copy-done.47, bf16[1024,256]{1,0:T(8,128)(2,1)S(1)} %bitcast.101), kind=kOutput, calls=%fused_computation.64 | convolution fusion | flops 1144520704 | bytes 3151872 | tf_op jit(solution)/shard_map/dot_general | solution.py:54
  56.0 0.1 reduce_sum.38
  56.2 0.1 convolution_convert_fusion.1
  56.3 19.5 %all_gather.3 = bf16[256,512]{1,0:T(8,128)(2,1)S(1)} all-gather(bf16[16,512]{1,0:T(8,128)(2,1)S(1)} %convolution_convert_fusion.1), channel_id=1, replica_groups=mesh['row'=16,'col'=16] {'col'}, dimensions={0}, use_global_device_ids=true | all-gather | bytes 278528 | tf_op jit(solution)/shard_map/all_gather | solution.py:102
  75.9 0.1 copy.19
  76.0 0.1 copy.20
  76.1 0.1 convolution_convert_fusion.2
  76.2 0.1 reshape.111
  76.3 0.1 fusion.17
  76.5 0.2 fusion.108
  76.7 0.3 fusion.18
  77.1 0.1 fusion.59
  77.2 0.1 broadcast_in_dim.2
  77.4 0.9 %add_convert_fusion = bf16[32,32,256]{2,1,0:T(8,128)(2,1)} fusion(f32[32,32,256]{2,1,0:T(8,128)S(1)} %bitcast.99, f32[32,32,256]{2,1,0:T(8,128)S(1)} %bitcast.100), kind=kLoop, calls=%fused_computation.74 | loop fusion | flops 524288 | bytes 2621440 | tf_op jit(solution)/shard_map/convert_element_type | solution.py:148
  (112 shorter events, 0.5 us)
Async XLA Ops:
  0.0 45.0 %copy-start = (bf16[1024,256]{1,0:T(8,128)(2,1)S(1)}, bf16[1024,256]{1,0:T(8,128)(2,1)}, u32[]{:S(2)}) copy-start(bf16[1024,256]{1,0:T(8,128)(2,1)} %param.21) | copy-start | bytes 1572868
  0.9 13.7 %collective-permute-start = (bf16[3,32,256]{2,1,0:T(8,128)(2,1)S(1)}, bf16[3,32,256]{2,1,0:T(8,128)(2,1)S(1)}, u32[]{:S(2)}, u32[]{:S(2)}) collective-permute-start(bf16[3,32,256]{2,1,0:T(8,128)(2,1)S(1)} %get-tuple-element.13), channel_id=1, source_target_pairs={{0,16},{16,32},{32,48},{48,64},{64,80},{80,96},{96,112},{112,128},... | collective-permute-start | bytes 147464 | tf_op jit(solution)/shard_map/ppermute | solution.py:16
  5.7 10.2 %collective-permute-start.1 = (bf16[3,32,256]{2,1,0:T(8,128)(2,1)S(1)}, bf16[3,32,256]{2,1,0:T(8,128)(2,1)S(1)}, u32[]{:S(2)}, u32[]{:S(2)}) collective-permute-start(bf16[3,32,256]{2,1,0:T(8,128)(2,1)S(1)} %get-tuple-element.12), channel_id=1, source_target_pairs={{16,0},{32,16},{48,32},{64,48},{80,64},{96,80},{112,96},{128,112},... | collective-permute-start | bytes 147464 | tf_op jit(solution)/shard_map/ppermute | solution.py:17
  15.9 7.1 %copy-start.1 = (bf16[35,32,256]{2,1,0:T(8,128)(2,1)}, bf16[35,32,256]{2,1,0:T(8,128)(2,1)S(1)}, u32[]{:S(2)}) copy-start(bf16[35,32,256]{2,1,0:T(8,128)(2,1)S(1)} %get-tuple-element.9) | copy-start | bytes 1720324
  15.9 7.1 %copy-start.4 = (bf16[38,32,256]{2,1,0:T(8,128)(2,1)}, bf16[38,32,256]{2,1,0:T(8,128)(2,1)S(1)}, u32[]{:S(2)}) copy-start(bf16[38,32,256]{2,1,0:T(8,128)(2,1)S(1)} %get-tuple-element.19) | copy-start | bytes 1867780
  16.8 13.0 %collective-permute-start.3 = (bf16[38,3,256]{2,1,0:T(4,128)(2,1)}, bf16[38,3,256]{2,1,0:T(4,128)(2,1)S(1)}, u32[]{:S(2)}, u32[]{:S(2)}) collective-permute-start(bf16[38,3,256]{2,1,0:T(4,128)(2,1)} %get-tuple-element.8), channel_id=1, source_target_pairs={{1,0},{2,1},{3,2},{4,3},{5,4},{6,5},{7,6},{8,7},{9,8},{10,9},{11,1... | collective-permute-start | bytes 175112 | tf_op jit(solution)/shard_map/ppermute | solution.py:17
  19.9 9.9 %collective-permute-start.2 = (bf16[38,3,256]{2,1,0:T(4,128)(2,1)}, bf16[38,3,256]{2,1,0:T(4,128)(2,1)}, u32[]{:S(2)}, u32[]{:S(2)}) collective-permute-start(bf16[38,3,256]{2,1,0:T(4,128)(2,1)} %get-tuple-element.7), channel_id=1, source_target_pairs={{0,1},{1,2},{2,3},{3,4},{4,5},{5,6},{6,7},{7,8},{8,9},{9,10},{10,1... | collective-permute-start | bytes 175112 | tf_op jit(solution)/shard_map/ppermute | solution.py:16
  26.9 2.9 %copy-start.10 = (f32[1,1,256]{2,1,0:T(1,128)S(1)}, f32[1,1,256]{2,1,0:T(1,128)}, u32[]{:S(2)}) copy-start(f32[1,1,256]{2,1,0:T(1,128)} %get-tuple-element.26) | copy-start | bytes 3076
  26.9 2.9 %copy-start.11 = (f32[1,1,256]{2,1,0:T(1,128)S(1)}, f32[1,1,256]{2,1,0:T(1,128)}, u32[]{:S(2)}) copy-start(f32[1,1,256]{2,1,0:T(1,128)} %get-tuple-element.27) | copy-start | bytes 3076
  26.9 2.9 %copy-start.12 = (f32[1,1,256]{2,1,0:T(1,128)S(1)}, f32[1,1,256]{2,1,0:T(1,128)}, u32[]{:S(2)}) copy-start(f32[1,1,256]{2,1,0:T(1,128)} %get-tuple-element.28) | copy-start | bytes 3076
  27.0 2.9 %copy-start.13 = (f32[1,1,256]{2,1,0:T(1,128)S(1)}, f32[1,1,256]{2,1,0:T(1,128)}, u32[]{:S(2)}) copy-start(f32[1,1,256]{2,1,0:T(1,128)} %get-tuple-element.29) | copy-start | bytes 3076
  27.0 2.9 %copy-start.14 = (f32[1,1,256]{2,1,0:T(1,128)S(1)}, f32[1,1,256]{2,1,0:T(1,128)}, u32[]{:S(2)}) copy-start(f32[1,1,256]{2,1,0:T(1,128)} %get-tuple-element.30) | copy-start | bytes 3076
  27.0 2.9 %copy-start.15 = (f32[1,1,256]{2,1,0:T(1,128)S(1)}, f32[1,1,256]{2,1,0:T(1,128)}, u32[]{:S(2)}) copy-start(f32[1,1,256]{2,1,0:T(1,128)} %get-tuple-element.31) | copy-start | bytes 3076
  27.0 2.9 %copy-start.16 = (f32[1,1,256]{2,1,0:T(1,128)S(1)}, f32[1,1,256]{2,1,0:T(1,128)}, u32[]{:S(2)}) copy-start(f32[1,1,256]{2,1,0:T(1,128)} %get-tuple-element.32) | copy-start | bytes 3076
  27.0 2.9 %copy-start.17 = (f32[1,1,256]{2,1,0:T(1,128)S(1)}, f32[1,1,256]{2,1,0:T(1,128)}, u32[]{:S(2)}) copy-start(f32[1,1,256]{2,1,0:T(1,128)} %get-tuple-element.33) | copy-start | bytes 3076
  27.0 2.9 %copy-start.18 = (f32[1,1,256]{2,1,0:T(1,128)S(1)}, f32[1,1,256]{2,1,0:T(1,128)}, u32[]{:S(2)}) copy-start(f32[1,1,256]{2,1,0:T(1,128)} %get-tuple-element.34) | copy-start | bytes 3076
  27.0 2.9 %copy-start.19 = (f32[1,1,256]{2,1,0:T(1,128)S(1)}, f32[1,1,256]{2,1,0:T(1,128)}, u32[]{:S(2)}) copy-start(f32[1,1,256]{2,1,0:T(1,128)} %get-tuple-element.35) | copy-start | bytes 3076
  27.0 2.9 %copy-start.20 = (f32[1,1,256]{2,1,0:T(1,128)S(1)}, f32[1,1,256]{2,1,0:T(1,128)}, u32[]{:S(2)}) copy-start(f32[1,1,256]{2,1,0:T(1,128)} %get-tuple-element.36) | copy-start | bytes 3076
  27.0 2.9 %copy-start.21 = (f32[1,1,256]{2,1,0:T(1,128)S(1)}, f32[1,1,256]{2,1,0:T(1,128)}, u32[]{:S(2)}) copy-start(f32[1,1,256]{2,1,0:T(1,128)} %get-tuple-element.37) | copy-start | bytes 3076
  27.0 2.9 %copy-start.22 = (f32[1,1,256]{2,1,0:T(1,128)S(1)}, f32[1,1,256]{2,1,0:T(1,128)}, u32[]{:S(2)}) copy-start(f32[1,1,256]{2,1,0:T(1,128)} %get-tuple-element.38) | copy-start | bytes 3076
  27.1 2.9 %copy-start.23 = (f32[1,1,256]{2,1,0:T(1,128)S(1)}, f32[1,1,256]{2,1,0:T(1,128)}, u32[]{:S(2)}) copy-start(f32[1,1,256]{2,1,0:T(1,128)} %get-tuple-element.39) | copy-start | bytes 3076
  27.1 2.9 %copy-start.24 = (f32[1,1,256]{2,1,0:T(1,128)S(1)}, f32[1,1,256]{2,1,0:T(1,128)}, u32[]{:S(2)}) copy-start(f32[1,1,256]{2,1,0:T(1,128)} %get-tuple-element.40) | copy-start | bytes 3076
  27.1 2.9 %copy-start.25 = (f32[1,1,256]{2,1,0:T(1,128)S(1)}, f32[1,1,256]{2,1,0:T(1,128)}, u32[]{:S(2)}) copy-start(f32[1,1,256]{2,1,0:T(1,128)} %get-tuple-element.41) | copy-start | bytes 3076
  27.1 2.9 %copy-start.26 = (f32[1,1,256]{2,1,0:T(1,128)S(1)}, f32[1,1,256]{2,1,0:T(1,128)}, u32[]{:S(2)}) copy-start(f32[1,1,256]{2,1,0:T(1,128)} %get-tuple-element.42) | copy-start | bytes 3076
  27.1 2.9 %copy-start.27 = (f32[1,1,256]{2,1,0:T(1,128)S(1)}, f32[1,1,256]{2,1,0:T(1,128)}, u32[]{:S(2)}) copy-start(f32[1,1,256]{2,1,0:T(1,128)} %get-tuple-element.43) | copy-start | bytes 3076
  27.1 2.9 %copy-start.28 = (f32[1,1,256]{2,1,0:T(1,128)S(1)}, f32[1,1,256]{2,1,0:T(1,128)}, u32[]{:S(2)}) copy-start(f32[1,1,256]{2,1,0:T(1,128)} %get-tuple-element.44) | copy-start | bytes 3076
  27.1 2.9 %copy-start.29 = (f32[1,1,256]{2,1,0:T(1,128)S(1)}, f32[1,1,256]{2,1,0:T(1,128)}, u32[]{:S(2)}) copy-start(f32[1,1,256]{2,1,0:T(1,128)} %get-tuple-element.45) | copy-start | bytes 3076
  27.1 2.9 %copy-start.30 = (f32[1,1,256]{2,1,0:T(1,128)S(1)}, f32[1,1,256]{2,1,0:T(1,128)}, u32[]{:S(2)}) copy-start(f32[1,1,256]{2,1,0:T(1,128)} %get-tuple-element.46) | copy-start | bytes 3076
  27.1 2.9 %copy-start.31 = (f32[1,1,256]{2,1,0:T(1,128)S(1)}, f32[1,1,256]{2,1,0:T(1,128)}, u32[]{:S(2)}) copy-start(f32[1,1,256]{2,1,0:T(1,128)} %get-tuple-element.47) | copy-start | bytes 3076
  45.1 11.1 %copy-start.6 = (bf16[256,512]{1,0:T(8,128)(2,1)S(1)}, bf16[256,512]{1,0:T(8,128)(2,1)}, u32[]{:S(2)}) copy-start(bf16[256,512]{1,0:T(8,128)(2,1)} %param.25) | copy-start | bytes 786436
  56.0 20.1 %copy-start.7 = (bf16[256,256]{1,0:T(8,128)(2,1)S(1)}, bf16[256,256]{1,0:T(8,128)(2,1)}, u32[]{:S(2)}) copy-start(bf16[256,256]{1,0:T(8,128)(2,1)} %param.24) | copy-start | bytes 393220
  56.0 21.1 %copy-start.8 = (bf16[256,256]{1,0:T(8,128)(2,1)S(1)}, bf16[256,256]{1,0:T(8,128)(2,1)}, u32[]{:S(2)}) copy-start(bf16[256,256]{1,0:T(8,128)(2,1)} %param.27) | copy-start | bytes 393220
  (20 other events, 53.5 us)
where the time goes:
time: 79.1 us; the launch traced here: 78.3 us
  other arithmetic  20.9 us (26%)
  blocking collectives  19.5 us (25%)
  starting transfers between devices  15.1 us (19%)
  matrix products  13.2 us (17%)
  local copies, waits for them, and re-layouts  8.61 us (11%)
  between operations  0.98 us (1%)
    all_gather x1, blocking collectives, shards(): band_keyval = lax.all_gather(keyval, 'col', axis=0, tiled=True)  19.5 us
    reduce_sum x1, other arithmetic, block_pass(): average = jnp.mean(convolved, axis=-1, keepdims=True)  13.4 us
    dot_general x1, matrix products, block_pass(): jnp.dot(hidden, w_reduce, preferred_element_type=jnp.float32) + b_reduce  10.9 us
    ppermute x2, starting transfers between devices, padded_2(): before = lax.ppermute(last, axis, up)  7.91 us
    ppermute x2, starting transfers between devices, padded_2(): after = lax.ppermute(leading, axis, down)  7.2 us
    mul x3, other arithmetic, block_pass(): padded[tap_row:tap_row + tile_rows, tap_col:tap_col + tile_cols]  4.79 us
    reshape x1, local copies, waits for them, and re-layouts, shards(): jnp.transpose(both_picked, (0, 1, 2, 4, 3, 5))  2.47 us
    transpose x1, local copies, waits for them, and re-layouts, shards(): jnp.transpose(both_picked, (0, 1, 2, 4, 3, 5))  1.76 us
  transfers between devices with their start and end apart: 4, of which 0 were waited for; matrix products, arithmetic and copies ran while one was open for 16% of the time, Pallas kernels for 0%

commit v1 on v0

--- a/solution.py
+++ b/solution.py
@@ -99,7 +99,9 @@
     pooled = pooled.astype(jnp.bfloat16).reshape(local_count, channels)
     queries = jnp.dot(pooled, w_query, preferred_element_type=jnp.float32).astype(jnp.bfloat16)
     keyval = jnp.dot(pooled, w_keyval, preferred_element_type=jnp.float32).astype(jnp.bfloat16)
-    band_keyval = lax.all_gather(keyval, "col", axis=0, tiled=True)
+    band_keyval = jnp.concatenate(
+        lax.all_to_all(jnp.stack([keyval] * lax.axis_size("col")), "col", 0, 0), axis=0
+    )
     columns = lax.axis_size("col")
     position = lax.axis_index("col")
     span_cols = region_side * columns

time: 79.1 us -> 63.4 us (0.80)
  blocking collectives: 19.5 us -> 0 us
  starting transfers between devices: 15.1 us -> 22 us
  other arithmetic: 20.9 us -> 15.7 us
  waiting for transfers between devices: 0.01 us -> 3.49 us
    all_gather x1 -> x0, blocking collectives: 19.5 us -> none  [shards(): band_keyval = lax.all_gather(keyval, 'col', axis=0, tiled=True)]
    all_to_all x0 -> x1, starting transfers between devices: none -> 6.85 us  [shards(): lax.all_to_all(jnp.stack([keyval] * lax.axis_size('col')), 'col', 0, 0)]
    reduce_sum x1, other arithmetic: 13.4 us -> 10.7 us  [block_pass(): average = jnp.mean(convolved, axis=-1, keepdims=True)]
    all_to_all x0 -> x1, waiting for transfers between devices: none -> 2.13 us  [shards(): lax.all_to_all(jnp.stack([keyval] * lax.axis_size('col')), 'col', 0, 0)]
    mul x3, other arithmetic: 4.79 us -> 2.89 us  [block_pass(): padded[tap_row:tap_row + tile_rows, tap_col:tap_col + tile_cols]]
    ppermute x2, waiting for transfers between devices: 0.01 us -> 1.29 us  [padded_2(): before = lax.ppermute(last, axis, up)]
  transfers between devices with their start and end apart: 4 -> 5, of which waited for: 0 -> 3; matrix products, arithmetic and copies ran while one was open for 16% -> 17% of each run, Pallas kernels for 0% -> 0%
where the time goes in v1:
time: 63.4 us; the launch traced here: 62.9 us
  starting transfers between devices  22 us (35%)
  other arithmetic  15.7 us (25%)
  matrix products  13.2 us (21%)
  local copies, waits for them, and re-layouts  8.18 us (13%)
  waiting for transfers between devices  3.49 us (6%)
    dot_general x1, matrix products, block_pass(): jnp.dot(hidden, w_reduce, preferred_element_type=jnp.float32) + b_reduce  10.9 us
    reduce_sum x1, other arithmetic, block_pass(): average = jnp.mean(convolved, axis=-1, keepdims=True)  10.7 us
    ppermute x2, starting transfers between devices, padded_2(): before = lax.ppermute(last, axis, up)  7.91 us
    ppermute x2, starting transfers between devices, padded_2(): after = lax.ppermute(leading, axis, down)  7.22 us
    all_to_all x1, starting transfers between devices, shards(): lax.all_to_all(jnp.stack([keyval] * lax.axis_size('col')), 'col', 0, 0)  6.85 us
    mul x3, other arithmetic, block_pass(): padded[tap_row:tap_row + tile_rows, tap_col:tap_col + tile_cols]  2.89 us
    reshape x1, local copies, waits for them, and re-layouts, shards(): jnp.transpose(both_picked, (0, 1, 2, 4, 3, 5))  2.21 us
    all_to_all x1, waiting for transfers between devices, shards(): lax.all_to_all(jnp.stack([keyval] * lax.axis_size('col')), 'col', 0, 0)  2.13 us
  transfers between devices with their start and end apart: 5, of which 3 were waited for; matrix products, arithmetic and copies ran while one was open for 17% of the time, Pallas kernels for 0%

profile of v1, /device:TPU:129, one launch (start us, length us, event | category | flops | bytes accessed | tf_op | source)
XLA Modules:
  0.0 62.9 jit_solution(1740060132887368057)
XLA Ops:
  0.0 0.9 %fusion.106 = (bf16[3,32,256]{2,1,0:T(8,128)(2,1)S(1)}, bf16[3,32,256]{2,1,0:T(8,128)(2,1)S(1)}) fusion(bf16[32,32,256]{2,1,0:T(8,128)(2,1)} %param.14), kind=kLoop, calls=%fused_computation.266 | loop fusion | bytes 196608 | tf_op jit(solution)/shard_map/slice | solution.py:15
  0.9 4.8 %collective-permute-start = (bf16[3,32,256]{2,1,0:T(8,128)(2,1)S(1)}, bf16[3,32,256]{2,1,0:T(8,128)(2,1)S(1)}, u32[]{:S(2)}, u32[]{:S(2)}) collective-permute-start(bf16[3,32,256]{2,1,0:T(8,128)(2,1)S(1)} %get-tuple-element.13), channel_id=1, source_target_pairs={{0,16},{16,32},{32,48},{48,64},{64,80},{80,96},{96,112},{112,128},... | collective-permute-start | bytes 147464 | tf_op jit(solution)/shard_map/ppermute | solution.py:16
  5.7 4.1 %collective-permute-start.1 = (bf16[3,32,256]{2,1,0:T(8,128)(2,1)S(1)}, bf16[3,32,256]{2,1,0:T(8,128)(2,1)S(1)}, u32[]{:S(2)}, u32[]{:S(2)}) collective-permute-start(bf16[3,32,256]{2,1,0:T(8,128)(2,1)S(1)} %get-tuple-element.12), channel_id=1, source_target_pairs={{16,0},{32,16},{48,32},{64,48},{80,64},{96,80},{112,96},{128,112},... | collective-permute-start | bytes 147464 | tf_op jit(solution)/shard_map/ppermute | solution.py:17
  9.8 0.9 %slice_convert_fusion.46 = (f32[1,1,256]{2,1,0:T(1,128)S(1)}, f32[1,1,256]{2,1,0:T(1,128)S(1)}, f32[1,1,256]{2,1,0:T(1,128)S(1)}, f32[1,1,256]{2,1,0:T(1,128)S(1...) fusion(bf16[7,7,256]{2,1,0:T(8,128)(2,1)} %param.15), kind=kLoop, calls=%fused_computation.229 | loop fusion | flops 2816 | bytes 16896 | tf_op jit(solution)/shard_map/mul | solution.py:39
  10.7 1.0 %slice_convert_fusion.48 = (f32[1,1,256]{2,1,0:T(1,128)S(1)}, f32[1,1,256]{2,1,0:T(1,128)S(1)}, f32[1,1,256]{2,1,0:T(1,128)S(1)}, f32[1,1,256]{2,1,0:T(1,128)S(1...) fusion(bf16[7,7,256]{2,1,0:T(8,128)(2,1)} %param.15), kind=kLoop, calls=%fused_computation.231 | loop fusion | flops 4864 | bytes 29184 | tf_op jit(solution)/shard_map/mul | solution.py:39
  11.7 1.0 %slice_convert_fusion.47 = (f32[1,1,256]{2,1,0:T(1,128)S(1)}, f32[1,1,256]{2,1,0:T(1,128)S(1)}, f32[1,1,256]{2,1,0:T(1,128)S(1)}, f32[1,1,256]{2,1,0:T(1,128)S(1...) fusion(bf16[7,7,256]{2,1,0:T(8,128)(2,1)} %param.15), kind=kLoop, calls=%fused_computation.230 | loop fusion | flops 4864 | bytes 29184 | tf_op jit(solution)/shard_map/mul | solution.py:39
  12.7 1.0 %fusion.67 = f32[4,4,8,127]{3,1,2,0:T(4,128)S(1)} fusion(f32[8,7,127,1]{2,0,1,3:T(8,128)} %bitcast.107, s32[4,4]{1,0:T(4,128)S(1)} %subtract_add_fusion), kind=kOutput, calls=%fused_computation.165 | convolution fusion | flops 1365616 | bytes 93536 | tf_op jit(solution)/shard_map/rso,hoc->hrsc/dot_general | solution.py:114
  13.8 1.2 %constant_dynamic-update-slice_fusion.3 = (bf16[35,32,256]{2,1,0:T(8,128)(2,1)S(1)}, bf16[38,32,256]{2,1,0:T(8,128)(2,1)S(1)}, bf16[35,32,256]{2,1,0:T(8,128)(2,1)S(1)}) fusion(bf16[35,32,256]{2,1,0:T(8,128)(2,1)S(1)} %get-tuple-element.16, bf16[32,32,256]{2,1,0:T(8,128)(2,1)} %param.14, bf16[38,32,256]{2,1,0:T(8,128)(2,1)S(1)} %get-tuple-element.17), kind=kLoop, calls=%fused_computation.171 | loop fusion | bytes 2097152 | tf_op jit(solution)/shard_map/concatenate | solution.py:18
  15.1 3.1 %collective-permute-start.3 = (bf16[38,3,256]{2,1,0:T(4,128)(2,1)S(1)}, bf16[38,3,256]{2,1,0:T(4,128)(2,1)S(1)}, u32[]{:S(2)}, u32[]{:S(2)}) collective-permute-start(bf16[38,3,256]{2,1,0:T(4,128)(2,1)S(1)} %get-tuple-element.8), channel_id=1, source_target_pairs={{1,0},{2,1},{3,2},{4,3},{5,4},{6,5},{7,6},{8,7},{9,8},{10,9},{11,1... | collective-permute-start | bytes 175112 | tf_op jit(solution)/shard_map/ppermute | solution.py:17
  18.3 3.1 %collective-permute-start.2 = (bf16[38,3,256]{2,1,0:T(4,128)(2,1)S(1)}, bf16[38,3,256]{2,1,0:T(4,128)(2,1)S(1)}, u32[]{:S(2)}, u32[]{:S(2)}) collective-permute-start(bf16[38,3,256]{2,1,0:T(4,128)(2,1)S(1)} %get-tuple-element.7), channel_id=1, source_target_pairs={{0,1},{1,2},{2,3},{3,4},{4,5},{5,6},{6,7},{7,8},{8,9},{9,10},{10,1... | collective-permute-start | bytes 175112 | tf_op jit(solution)/shard_map/ppermute | solution.py:16
  21.5 1.3 %collective-permute-done.2 = bf16[38,3,256]{2,1,0:T(4,128)(2,1)S(1)} collective-permute-done((bf16[38,3,256]{2,1,0:T(4,128)(2,1)S(1)}, bf16[38,3,256]{2,1,0:T(4,128)(2,1)S(1)}, u32[]{:S(2)}, u32[]{:S(2)}) %collective-permute-start.2) | collective-permute-done | bytes 58400 | tf_op jit(solution)/shard_map/ppermute | solution.py:16
  22.8 10.7 %fusion.104 = (f32[32,32]{1,0:T(8,128)S(1)}, f32[32,32,256]{2,1,0:T(8,128)S(1)}) fusion(f32[256]{0:T(256)S(1)} %copy-done.7, f32[256]{0:T(256)S(1)} %bitcast.117, bf16[38,3,256]{2,1,0:T(4,128)(2,1)S(1)} %collective-permute-done.3, bf16[38,32,256]{2,1,0:T(8,128)(2,1)S(1)} %get-tuple-element.19, f32[256]{0:T(256)S(1)} %bitcast.118, f32[256]{0:T(256)S(1)} %bitcast.120, ...), kind=kLoop, calls=%fused_computation.264 | loop fusion | flops 71826432 | bytes 5513216 | tf_op jit(solution)/shard_map/reduce_sum | solution.py:43
  33.6 0.4 multiply_reduce_fusion
  34.0 0.3 add_convert_fusion.1
  34.4 10.9 %fusion.14 = f32[1024,256]{1,0:T(8,128)S(1)} fusion(bf16[1024,256]{1,0:T(8,128)(2,1)S(1)} %copy-done, bf16[1024,256]{1,0:T(8,128)(2,1)S(1)} %bitcast.104, bf16[256,1024]{1,0:T(8,128)(2,1)} %param.19, f32[1024]{0:T(1024)S(1)} %copy-done.10, f32[256]{0:T(256)S(1)} %copy-done.11, f32[256]{0:T(256)S(1)} %copy-done.12, bf16[1024,256]{1,0:T(8,128)(2,1)S(1)} %bitcast.102), kind=kOutput, calls=%fused_computation.64 | convolution fusion | flops 1144520704 | bytes 3151872 | tf_op jit(solution)/shard_map/dot_general | solution.py:54
  45.5 0.1 convolution_convert_fusion.1
  45.6 0.8 %stack.2 = bf16[16,16,512]{2,1,0:T(8,128)(2,1)} broadcast(bf16[16,512]{1,0:T(8,128)(2,1)S(1)} %convolution_convert_fusion.1), dimensions={1,2} | broadcast | bytes 278528 | tf_op jit(solution)/shard_map/stack | solution.py:103
  46.4 6.9 %all-to-all-start = ((bf16[16,16,512]{2,1,0:T(8,128)(2,1)}), bf16[16,16,512]{2,1,0:T(8,128)(2,1)S(1)}, u32[]{:S(2)}, u32[]{:S(2)}) async-start(bf16[16,16,512]{2,1,0:T(8,128)(2,1)} %stack.2), calls=%async_computation | async-start | bytes 524288 | tf_op jit(solution)/shard_map/all_to_all | solution.py:103
  53.2 0.4 convolution_bitcast_fusion
  53.7 0.6 copy.21
  54.3 1.7 %copy.22 = f32[8,4,4,16,4,4]{0,5,4,3,2,1:T(4,128)} copy(f32[8,4,4,16,4,4]{0,5,3,4,2,1:T(4,128)S(1)} %bitcast.97) | data formatting | bytes 262144 | tf_op jit(solution)/shard_map/transpose | solution.py:127
  56.0 2.2 %copy.23 = f32[8,16,256]{2,1,0:T(8,128)S(1)} copy(f32[8,16,256]{0,2,1:T(8,128)} %bitcast.98) | data formatting | bytes 262144 | tf_op jit(solution)/shard_map/reshape | solution.py:127
  58.3 0.1 convolution_convert_fusion.2
  58.4 0.1 reshape.117
  58.5 2.1 %all-to-all-done = bf16[16,16,512]{2,1,0:T(8,128)(2,1)S(1)} async-done(((bf16[16,16,512]{2,1,0:T(8,128)(2,1)}), bf16[16,16,512]{2,1,0:T(8,128)(2,1)S(1)}, u32[]{:S(2)}, u32[]{:S(2)}) %all-to-all-start) | async-done | bytes 262176 | tf_op jit(solution)/shard_map/all_to_all | solution.py:103
  60.8 0.1 copy.19
  60.9 0.1 fusion.17
  61.0 0.2 fusion.108
  61.2 0.3 fusion.18
  61.6 0.1 fusion.59
  61.8 0.1 broadcast_in_dim.2
  61.9 1.0 %add_convert_fusion = bf16[32,32,256]{2,1,0:T(8,128)(2,1)} fusion(f32[32,32,256]{2,1,0:T(8,128)S(1)} %bitcast.100, f32[32,32,256]{2,1,0:T(8,128)S(1)} %bitcast.101), kind=kLoop, calls=%fused_computation.74 | loop fusion | flops 524288 | bytes 2621440 | tf_op jit(solution)/shard_map/convert_element_type | solution.py:150
  (44 shorter events, 0.7 us)
Async XLA Ops:
  0.0 34.4 %copy-start = (bf16[1024,256]{1,0:T(8,128)(2,1)S(1)}, bf16[1024,256]{1,0:T(8,128)(2,1)}, u32[]{:S(2)}) copy-start(bf16[1024,256]{1,0:T(8,128)(2,1)} %param.21) | copy-start | bytes 1572868
  0.0 22.8 %copy-start.3 = (bf16[32,32,256]{2,1,0:T(8,128)(2,1)S(1)}, bf16[32,32,256]{2,1,0:T(8,128)(2,1)}, u32[]{:S(2)}) copy-start(bf16[32,32,256]{2,1,0:T(8,128)(2,1)} %param.14) | copy-start | bytes 1572868
  0.0 22.8 %copy-start.7 = (f32[256]{0:T(256)S(1)}, f32[256]{0:T(256)}, u32[]{:S(2)}) copy-start(f32[256]{0:T(256)} %param.16) | copy-start | bytes 3076
  0.9 12.8 %collective-permute-start = (bf16[3,32,256]{2,1,0:T(8,128)(2,1)S(1)}, bf16[3,32,256]{2,1,0:T(8,128)(2,1)S(1)}, u32[]{:S(2)}, u32[]{:S(2)}) collective-permute-start(bf16[3,32,256]{2,1,0:T(8,128)(2,1)S(1)} %get-tuple-element.13), channel_id=1, source_target_pairs={{0,16},{16,32},{32,48},{48,64},{64,80},{80,96},{96,112},{112,128},... | collective-permute-start | bytes 147464 | tf_op jit(solution)/shard_map/ppermute | solution.py:16
  5.7 9.3 %collective-permute-start.1 = (bf16[3,32,256]{2,1,0:T(8,128)(2,1)S(1)}, bf16[3,32,256]{2,1,0:T(8,128)(2,1)S(1)}, u32[]{:S(2)}, u32[]{:S(2)}) collective-permute-start(bf16[3,32,256]{2,1,0:T(8,128)(2,1)S(1)} %get-tuple-element.12), channel_id=1, source_target_pairs={{16,0},{32,16},{48,32},{64,48},{80,64},{96,80},{112,96},{128,112},... | collective-permute-start | bytes 147464 | tf_op jit(solution)/shard_map/ppermute | solution.py:17
  15.1 6.4 %collective-permute-start.3 = (bf16[38,3,256]{2,1,0:T(4,128)(2,1)S(1)}, bf16[38,3,256]{2,1,0:T(4,128)(2,1)S(1)}, u32[]{:S(2)}, u32[]{:S(2)}) collective-permute-start(bf16[38,3,256]{2,1,0:T(4,128)(2,1)S(1)} %get-tuple-element.8), channel_id=1, source_target_pairs={{1,0},{2,1},{3,2},{4,3},{5,4},{6,5},{7,6},{8,7},{9,8},{10,9},{11,1... | collective-permute-start | bytes 175112 | tf_op jit(solution)/shard_map/ppermute | solution.py:17
  18.3 4.5 %collective-permute-start.2 = (bf16[38,3,256]{2,1,0:T(4,128)(2,1)S(1)}, bf16[38,3,256]{2,1,0:T(4,128)(2,1)S(1)}, u32[]{:S(2)}, u32[]{:S(2)}) collective-permute-start(bf16[38,3,256]{2,1,0:T(4,128)(2,1)S(1)} %get-tuple-element.7), channel_id=1, source_target_pairs={{0,1},{1,2},{2,3},{3,4},{4,5},{5,6},{6,7},{7,8},{8,9},{9,10},{10,1... | collective-permute-start | bytes 175112 | tf_op jit(solution)/shard_map/ppermute | solution.py:16
  22.8 11.2 %copy-start.8 = (f32[256]{0:T(256)S(1)}, f32[256]{0:T(256)}, u32[]{:S(2)}) copy-start(f32[256]{0:T(256)} %param.18) | copy-start | bytes 3076
  22.8 11.2 %copy-start.9 = (f32[256]{0:T(256)S(1)}, f32[256]{0:T(256)}, u32[]{:S(2)}) copy-start(f32[256]{0:T(256)} %param.17) | copy-start | bytes 3076
  33.5 0.8 %copy-start.10 = (f32[1024]{0:T(1024)S(1)}, f32[1024]{0:T(1024)}, u32[]{:S(2)}) copy-start(f32[1024]{0:T(1024)} %param.20) | copy-start | bytes 12292
  33.6 0.8 %copy-start.11 = (f32[256]{0:T(256)S(1)}, f32[256]{0:T(256)}, u32[]{:S(2)}) copy-start(f32[256]{0:T(256)} %param.22) | copy-start | bytes 3076
  33.6 0.8 %copy-start.12 = (f32[256]{0:T(256)S(1)}, f32[256]{0:T(256)}, u32[]{:S(2)}) copy-start(f32[256]{0:T(256)} %param.23) | copy-start | bytes 3076
  34.4 11.1 %copy-start.4 = (bf16[256,512]{1,0:T(8,128)(2,1)S(1)}, bf16[256,512]{1,0:T(8,128)(2,1)}, u32[]{:S(2)}) copy-start(bf16[256,512]{1,0:T(8,128)(2,1)} %param.25) | copy-start | bytes 786436
  45.3 7.9 %copy-start.1 = (f32[1024,256]{1,0:T(8,128)}, f32[1024,256]{1,0:T(8,128)S(1)}, u32[]{:S(2)}) copy-start(f32[1024,256]{1,0:T(8,128)S(1)} %fusion.14) | copy-start | bytes 3145732
  46.4 14.3 %all-to-all-start = ((bf16[16,16,512]{2,1,0:T(8,128)(2,1)}), bf16[16,16,512]{2,1,0:T(8,128)(2,1)S(1)}, u32[]{:S(2)}, u32[]{:S(2)}) async-start(bf16[16,16,512]{2,1,0:T(8,128)(2,1)} %stack.2), calls=%async_computation | async-start | bytes 524288 | tf_op jit(solution)/shard_map/all_to_all | solution.py:103
  56.0 2.2 %copy-start.5 = (bf16[256,256]{1,0:T(8,128)(2,1)S(1)}, bf16[256,256]{1,0:T(8,128)(2,1)}, u32[]{:S(2)}) copy-start(bf16[256,256]{1,0:T(8,128)(2,1)} %param.24) | copy-start | bytes 393220
  56.0 5.6 %copy-start.6 = (bf16[256,256]{1,0:T(8,128)(2,1)S(1)}, bf16[256,256]{1,0:T(8,128)(2,1)}, u32[]{:S(2)}) copy-start(bf16[256,256]{1,0:T(8,128)(2,1)} %param.27) | copy-start | bytes 393220
  58.3 3.6 %copy-start.2 = (f32[1024,256]{1,0:T(8,128)S(1)}, f32[1024,256]{1,0:T(8,128)}, u32[]{:S(2)}) copy-start(f32[1024,256]{1,0:T(8,128)} %copy-done.1) | copy-start | bytes 3145732
